TPU v7x, 128 devices: a whole 4x4x4 slice. The times are simulated.
128 devices in a mesh: dp: 16 (over y, x_lo, core), ctx: 8 (over z, x_hi).
Axes of the slice: x: 4 (x_hi: 2, x_lo: 2; x = x_hi * 2 + x_lo), y: 4, z: 4, core: 2. Of those that a mesh axis runs over, the one named last changes fastest.
Arguments:
- query_in: bfloat16 [32768, 2048], P(('dp', 'ctx')), may hold values from -16 to 16
- key_in: bfloat16 [32768, 512], P(('dp', 'ctx')), may hold values from -16 to 16
- value_in: bfloat16 [32768, 512], P(('dp', 'ctx')), may hold values from -6 to 6
- grad_out: bfloat16 [32768, 2048], P(('dp', 'ctx')), may hold values from -6 to 6
- target: int32 [32768], P(('dp', 'ctx')), may hold values from 0 to 32767, as said below
- span_order: int32 [16, 16], P('dp'), may hold values from 0 to 15, each once within a row
- doc_ids: int32 [16, 2048], P('dp', 'ctx'), may hold values from 0 to 7, never falling along the last dimension, each value on 1 to 1024 neighbouring positions
Outputs:
- grad_query: float32 [32768, 2048], P(('dp', 'ctx'))
- grad_key: float32 [32768, 512], P(('dp', 'ctx'))
- grad_value: float32 [32768, 512], P(('dp', 'ctx'))
Inputs may be any that keep to these rules, and one draw needn't show every extreme that they name: target is a permutation of the 32768 packed rows; of the 256 rows of one device at most 4 go to any one block of 256 packed rows, and exactly 4 go to some block. `span_order`: each row names every span once. `doc_ids`: each document is one run of 1 to 1024 positions; numbers never fall along a pack.
All inputs are finite; a program needn't handle non-finite values.
Results may differ from a plain program's by a relative error of at most 0.035.
Values may be sent and summed in bfloat16 or wider, within the bound.
No kernel may reach another device: no remote copies, remote signals or barrier semaphores. Data moves between devices by JAX's collectives and lax.ppermute only.
A program may use at most 128 MiB of HBM per device.

v0:
```python
import jax
import jax.numpy as jnp
from jax import lax
from jax.sharding import PartitionSpec as P

HQ = 16
HK = 4
DH = 128


block_keys = 512


def visible(query_pos, query_doc, key_pos, key_doc):
    return (key_pos[None, :] <= query_pos[:, None]) & (key_doc[None, :] == query_doc[:, None])


def masked_scores(query_blk, key_blk, allowed):
    raw_scores = jnp.einsum(
        "qhgd,khd->hgqk", query_blk, key_blk, preferred_element_type=jnp.float32
    ) * DH ** (-0.5)
    return jnp.where(allowed[None, None], raw_scores, -jnp.inf)


def grad_terms(query_blk, grad_blk, lse_blk, delta_blk, key_blk, value_blk, allowed):
    scores = masked_scores(query_blk, key_blk, allowed)
    probs = jnp.exp(scores - lse_blk[..., None])
    probs_low = probs.astype(jnp.bfloat16)
    dprobs = jnp.einsum("qhgd,khd->hgqk", grad_blk, value_blk, preferred_element_type=jnp.float32)
    dscore_low = (probs * (dprobs - delta_blk[..., None])).astype(jnp.bfloat16)
    return (probs_low, dscore_low)


def local(query_in, key_in, value_in, grad_out, target, span_order, doc_ids):
    local_rows = query_in.shape[0]
    devices = lax.axis_size(("dp", "ctx"))
    ctx_size = lax.axis_size("ctx")
    capacity = local_rows // devices + 2
    groups = HQ // HK
    score_scale = DH ** (-0.5)
    owners = target // local_rows
    onehot = (owners[:, None] == jnp.arange(devices, dtype=jnp.int32)[None, :]).astype(jnp.int32)
    earlier = jnp.cumsum(onehot, axis=0) - onehot
    slot_ids = owners * capacity + jnp.sum(earlier * onehot, axis=1)

    def bucket(values, filler):
        holder = jnp.full((devices * capacity,) + values.shape[1:], filler, values.dtype)
        return holder.at[slot_ids].set(values).reshape((devices, capacity) + values.shape[1:])

    got_query, got_key, got_value, got_grad, got_place = (
        lax.all_to_all(bucket(query_in, 0), ("dp", "ctx"), split_axis=0, concat_axis=0, tiled=True),
        lax.all_to_all(bucket(key_in, 0), ("dp", "ctx"), split_axis=0, concat_axis=0, tiled=True),
        lax.all_to_all(bucket(value_in, 0), ("dp", "ctx"), split_axis=0, concat_axis=0, tiled=True),
        lax.all_to_all(bucket(grad_out, 0), ("dp", "ctx"), split_axis=0, concat_axis=0, tiled=True),
        lax.all_to_all(
            bucket(target % local_rows, -1), ("dp", "ctx"), split_axis=0, concat_axis=0, tiled=True
        ),
    )
    arrived = got_place.reshape(-1)
    landing = jnp.where(arrived >= 0, arrived, local_rows)

    def unpack(values):
        values = values.reshape((devices * capacity,) + values.shape[2:])
        return (
            jnp.zeros((local_rows,) + values.shape[1:], values.dtype)
            .at[landing]
            .set(values, mode="drop")
        )

    query = unpack(got_query)
    key_rows = unpack(got_key)
    value_rows = unpack(got_value)
    grad_rows = unpack(got_grad)
    span_rows = local_rows // 2
    span_seq = span_order[0]
    pack_len = local_rows * ctx_size
    positions = (
        span_seq[:, None] * span_rows + jnp.arange(span_rows, dtype=jnp.int32)[None, :]
    ).reshape(-1)
    ctx_index = lax.axis_index("ctx")
    own_pos = lax.dynamic_slice_in_dim(positions, ctx_index * local_rows, local_rows)
    keys_all, values_all, seq_docs = (
        lax.all_gather(key_rows, "ctx", axis=0, tiled=True),
        lax.all_gather(value_rows, "ctx", axis=0, tiled=True),
        lax.all_gather(doc_ids[0], "ctx", axis=0, tiled=True),
    )
    doc_all = seq_docs.reshape(2 * ctx_size, span_rows)[span_seq].reshape(-1)
    own_docs = lax.dynamic_slice_in_dim(doc_all, ctx_index * local_rows, local_rows)
    query_heads = query.reshape(local_rows, HK, groups, DH)
    grad_heads = grad_rows.reshape(local_rows, HK, groups, DH)
    key_heads = keys_all.reshape(pack_len, HK, DH)
    value_heads = values_all.reshape(pack_len, HK, DH)
    num_blocks = pack_len // block_keys

    def key_block(block_index):
        first_key = block_index * block_keys
        return (
            lax.dynamic_slice_in_dim(key_heads, first_key, block_keys),
            lax.dynamic_slice_in_dim(value_heads, first_key, block_keys),
            lax.dynamic_slice_in_dim(positions, first_key, block_keys),
            lax.dynamic_slice_in_dim(doc_all, first_key, block_keys),
        )

    def stats_step(block_index, carry):
        key_blk, value_blk, key_pos, key_doc = key_block(block_index)
        allowed = visible(own_pos, own_docs, key_pos, key_doc)
        running_max, running_sum = carry
        scores = masked_scores(query_heads, key_blk, allowed)
        new_max = jnp.maximum(running_max, jnp.max(scores, axis=-1))
        rescale = jnp.exp(running_max - new_max)
        running_sum = running_sum * rescale + jnp.sum(jnp.exp(scores - new_max[..., None]), axis=-1)
        return (new_max, running_sum)

    start_stats = (
        jnp.full((HK, groups, local_rows), -1e30, jnp.float32),
        jnp.zeros((HK, groups, local_rows), jnp.float32),
    )
    running_max, running_sum = lax.fori_loop(0, num_blocks, stats_step, start_stats)
    log_norm = running_max + jnp.log(running_sum)

    def output_step(block_index, carry):
        key_blk, value_blk, key_pos, key_doc = key_block(block_index)
        allowed = visible(own_pos, own_docs, key_pos, key_doc)
        scores = masked_scores(query_heads, key_blk, allowed)
        probs_low = jnp.exp(scores - log_norm[..., None]).astype(jnp.bfloat16)
        return carry + jnp.einsum(
            "hgqk,khd->qhgd", probs_low, value_blk, preferred_element_type=jnp.float32
        )

    summed = lax.fori_loop(
        0, num_blocks, output_step, jnp.zeros((local_rows, HK, groups, DH), jnp.float32)
    )
    attended_low = summed.astype(jnp.bfloat16)
    delta = jnp.sum(
        grad_heads.astype(jnp.float32) * attended_low.astype(jnp.float32), axis=-1
    ).transpose(1, 2, 0)

    def back_step(block_index, carry):
        key_blk, value_blk, key_pos, key_doc = key_block(block_index)
        allowed = visible(own_pos, own_docs, key_pos, key_doc)
        dquery, dkey_all, dvalue_all = carry
        probs_low, dscore_low = grad_terms(
            query_heads, grad_heads, log_norm, delta, key_blk, value_blk, allowed
        )
        dquery = dquery + jnp.einsum(
            "hgqk,khd->qhgd", dscore_low, key_blk, preferred_element_type=jnp.float32
        )
        dkey = (
            jnp.einsum(
                "hgqk,qhgd->khd", dscore_low, query_heads, preferred_element_type=jnp.float32
            )
            * score_scale
        )
        dvalue = jnp.einsum(
            "hgqk,qhgd->khd", probs_low, grad_heads, preferred_element_type=jnp.float32
        )
        first_key = block_index * block_keys
        dkey_all = lax.dynamic_update_slice_in_dim(
            dkey_all, dkey.reshape(block_keys, HK * DH), first_key, 0
        )
        dvalue_all = lax.dynamic_update_slice_in_dim(
            dvalue_all, dvalue.reshape(block_keys, HK * DH), first_key, 0
        )
        return (dquery, dkey_all, dvalue_all)

    start_back = (
        jnp.zeros((local_rows, HK, groups, DH), jnp.float32),
        jnp.zeros((pack_len, HK * DH), jnp.float32),
        jnp.zeros((pack_len, HK * DH), jnp.float32),
    )
    dquery, dkey_all, dvalue_all = lax.fori_loop(0, num_blocks, back_step, start_back)
    dkey_own, dvalue_own = (
        lax.psum_scatter(dkey_all, "ctx", scatter_dimension=0, tiled=True),
        lax.psum_scatter(dvalue_all, "ctx", scatter_dimension=0, tiled=True),
    )
    dquery_full = (dquery * score_scale).reshape(local_rows, HQ * DH)
    source_rows = jnp.where(arrived >= 0, arrived, 0)

    def outgoing(values):
        return values[source_rows].reshape((devices, capacity) + values.shape[1:])

    back_query, back_key, back_value = (
        lax.all_to_all(
            outgoing(dquery_full).astype(jnp.bfloat16),
            ("dp", "ctx"),
            split_axis=0,
            concat_axis=0,
            tiled=True,
        ).astype(jnp.float32),
        lax.all_to_all(
            outgoing(dkey_own).astype(jnp.bfloat16),
            ("dp", "ctx"),
            split_axis=0,
            concat_axis=0,
            tiled=True,
        ).astype(jnp.float32),
        lax.all_to_all(
            outgoing(dvalue_own).astype(jnp.bfloat16),
            ("dp", "ctx"),
            split_axis=0,
            concat_axis=0,
            tiled=True,
        ).astype(jnp.float32),
    )

    def picked(values):
        return values.reshape((devices * capacity,) + values.shape[2:])[slot_ids]

    return (picked(back_query), picked(back_key), picked(back_value))


def solution(mesh):
    placed = (
        P(("dp", "ctx"), None),
        P(("dp", "ctx"), None),
        P(("dp", "ctx"), None),
        P(("dp", "ctx"), None),
        P(("dp", "ctx")),
        P("dp", None),
        P("dp", "ctx"),
    )
    return jax.shard_map(
        local,
        mesh=mesh,
        in_specs=placed,
        out_specs=(P(("dp", "ctx"), None), P(("dp", "ctx"), None), P(("dp", "ctx"), None)),
        check_vma=False,
    )
```

profile of v0, /device:TPU:1, one launch (start us, length us, event | category | flops | bytes accessed | tf_op | source)
XLA Modules:
  0.0 583.2 jit_solution(5741435279528771438)
XLA Ops:
  10.6 11.5 %all-to-all-start = ((s32[128,1,4]{2,1,0:T(1,128)}), s32[128,1,4]{2,1,0:T(1,128)S(1)}, u32[]{:S(2)}, u32[]{:S(2)}) async-start(s32[128,1,4]{2,1,0:T(1,128)} %bitcast.4), calls=%async_computation | async-start | bytes 131072 | tf_op jit(solution)/shard_map/all_to_all | solution.py:55
  25.1 6.8 %all-to-all-done = s32[128,1,4]{2,1,0:T(1,128)S(1)} async-done(((s32[128,1,4]{2,1,0:T(1,128)}), s32[128,1,4]{2,1,0:T(1,128)S(1)}, u32[]{:S(2)}, u32[]{:S(2)}) %all-to-all-start) | async-done | bytes 2080 | tf_op jit(solution)/shard_map/all_to_all | solution.py:55
  39.1 11.0 %all-to-all-done.3 = bf16[128,4,512]{2,1,0:T(4,128)(2,1)S(1)} async-done(((bf16[128,4,512]{2,1,0:T(4,128)(2,1)}), bf16[128,4,512]{2,1,0:T(4,128)(2,1)S(1)}, u32[]{:S(2)}, u32[]{:S(2)}) %all-to-all-start.3) | async-done | bytes 524320 | tf_op jit(solution)/shard_map/all_to_all | solution.py:53
  59.8 8.3 %all-to-all-done.1 = bf16[128,4,512]{2,1,0:T(4,128)(2,1)S(1)} async-done(((bf16[128,4,512]{2,1,0:T(4,128)(2,1)}), bf16[128,4,512]{2,1,0:T(4,128)(2,1)S(1)}, u32[]{:S(2)}, u32[]{:S(2)}) %all-to-all-start.1) | async-done | bytes 524320 | tf_op jit(solution)/shard_map/all_to_all | solution.py:52
  87.4 18.2 %all-to-all-done.2 = bf16[128,4,2048]{2,1,0:T(4,128)(2,1)S(1)} async-done(((bf16[128,4,2048]{2,1,0:T(4,128)(2,1)}), bf16[128,4,2048]{2,1,0:T(4,128)(2,1)S(1)}, u32[]{:S(2)}, u32[]{:S(2)}) %all-to-all-start.2) | async-done | bytes 2097184 | tf_op jit(solution)/shard_map/all_to_all | solution.py:51
  111.0 47.5 %all-gather = s32[1,2048]{1,0:T(1,128)S(1)} all-gather(s32[1,256]{1,0:T(1,128)S(1)} %copy-done.9), channel_id=2, replica_groups=mesh['dp'=16,'ctx'=8] {'ctx'}, dimensions={1}, use_global_device_ids=true | all-gather | bytes 9216 | tf_op jit(solution)/shard_map/all_gather | solution.py:85
  175.4 5.6 scatter_custom_fusion.8
  190.4 18.2 %while.48 = (s32[]{:T(128)}, f32[4,4,256]{2,1,0:T(4,128)S(1)}, f32[4,4,256]{2,1,0:T(4,128)S(1)}, s32[2048]{0:T(1024)S(1)}, s32[256]{0:T(256)S(1)}, /*index=5*/s3...) while((s32[]{:T(128)}, f32[4,4,256]{2,1,0:T(4,128)S(1)}, ...), condition=%wide.region_13.14_spmd.clone, body=%wide.region_10.13_spmd.clone.sunk | while | flops 551964672 | bytes 18970824 | solution.py:118
  208.6 8.1 %all-gather.6.cloned.1.call-done = bf16[2048,512]{1,0:T(8,128)(2,1)} async-done(((bf16[256,512]{1,0:T(8,128)(2,1)}), bf16[2048,512]{1,0:T(8,128)(2,1)}) %all-gather.6.cloned.1.call-update) | async-done | bytes 2097168 | tf_op jit(solution)/shard_map/all_gather | solution.py:84
  220.6 23.9 %while.49 = (s32[]{:T(128)}, f32[256,4,4,128]{0,3,2,1:T(8,128)}, bf16[2048,4,128]{0,2,1:T(8,128)(2,1)}, s32[2048]{0:T(1024)S(1)}, s32[256]{0:T(256)S(1)}, /*inde...) while((s32[]{:T(128)}, f32[256,4,4,128]{0,3,2,1:T(8,128)}, ...), condition=%wide.region_17.18_spmd.clone, body=%wide.region_16.17_spmd.clone.sunk | while | flops 1083572224 | bytes 6586060 | solution.py:130
  226.4 5.8 bitcast_add_fusion.4
  232.6 5.8 bitcast_add_fusion.4
  238.7 5.8 bitcast_add_fusion.4
  251.3 100.7 %while.50 = (s32[]{:T(128)}, f32[256,4,4,128]{0,3,2,1:T(8,128)}, f32[2048,512]{1,0:T(8,128)}, f32[2048,512]{1,0:T(8,128)}, bf16[2048,4,128]{2,0,1:T(8,128)(2,1)}...) while((s32[]{:T(128)}, f32[256,4,4,128]{0,3,2,1:T(8,128)}, ...), condition=%wide.region_20.21_spmd.clone, body=%wide.region_19.20_spmd.clone.sunk | while | flops 2707030016 | bytes 100596096 | solution.py:171
  258.5 6.0 %fusion.121 = bf16[4,4,256,512]{2,3,1,0:T(8,128)(2,1)} fusion(f32[4,512,256,4]{2,1,3,0:T(8,128)S(1)} %fusion.120, f32[4,4,256]{2,1,0:T(4,128)S(1)} %get-tuple-element.1203, f32[4,4,256]{2,1,0:T(4,128)S(1)} %get-tuple-element.1200, pred[256,512]{0,1:T(8,128)(4,1)S(1)} %compare_and_fusion.8, bf16[256,4,4,128]{0,3,2,1:T(8,128)(2,1)} %copy-done.4, ...), kind=kOutput, calls=%fused_computation.48.clone.1 | convolution fusion | flops 549453824 | bytes 14319620 | tf_op jit(solution)/shard_map/while/body/eval_jaxpr/qhgd,khd->hgqk/dot_general | solution.py:29
  283.5 6.0 %fusion.121 = bf16[4,4,256,512]{2,3,1,0:T(8,128)(2,1)} fusion(f32[4,512,256,4]{2,1,3,0:T(8,128)S(1)} %fusion.120, f32[4,4,256]{2,1,0:T(4,128)S(1)} %get-tuple-element.1203, f32[4,4,256]{2,1,0:T(4,128)S(1)} %get-tuple-element.1200, pred[256,512]{0,1:T(8,128)(4,1)S(1)} %compare_and_fusion.8, bf16[256,4,4,128]{0,3,2,1:T(8,128)(2,1)} %copy-done.4, ...), kind=kOutput, calls=%fused_computation.48.clone.1 | convolution fusion | flops 549453824 | bytes 14319620 | tf_op jit(solution)/shard_map/while/body/eval_jaxpr/qhgd,khd->hgqk/dot_general | solution.py:29
  308.6 6.0 %fusion.121 = bf16[4,4,256,512]{2,3,1,0:T(8,128)(2,1)} fusion(f32[4,512,256,4]{2,1,3,0:T(8,128)S(1)} %fusion.120, f32[4,4,256]{2,1,0:T(4,128)S(1)} %get-tuple-element.1203, f32[4,4,256]{2,1,0:T(4,128)S(1)} %get-tuple-element.1200, pred[256,512]{0,1:T(8,128)(4,1)S(1)} %compare_and_fusion.8, bf16[256,4,4,128]{0,3,2,1:T(8,128)(2,1)} %copy-done.4, ...), kind=kOutput, calls=%fused_computation.48.clone.1 | convolution fusion | flops 549453824 | bytes 14319620 | tf_op jit(solution)/shard_map/while/body/eval_jaxpr/qhgd,khd->hgqk/dot_general | solution.py:29
  333.7 6.0 %fusion.121 = bf16[4,4,256,512]{2,3,1,0:T(8,128)(2,1)} fusion(f32[4,512,256,4]{2,1,3,0:T(8,128)S(1)} %fusion.120, f32[4,4,256]{2,1,0:T(4,128)S(1)} %get-tuple-element.1203, f32[4,4,256]{2,1,0:T(4,128)S(1)} %get-tuple-element.1200, pred[256,512]{0,1:T(8,128)(4,1)S(1)} %compare_and_fusion.8, bf16[256,4,4,128]{0,3,2,1:T(8,128)(2,1)} %copy-done.4, ...), kind=kOutput, calls=%fused_computation.48.clone.1 | convolution fusion | flops 549453824 | bytes 14319620 | tf_op jit(solution)/shard_map/while/body/eval_jaxpr/qhgd,khd->hgqk/dot_general | solution.py:29
  359.3 6.8 %all-to-all-start.5 = ((bf16[128,4,2048]{2,1,0:T(4,128)(2,1)}), bf16[128,4,2048]{2,1,0:T(4,128)(2,1)S(1)}, u32[]{:S(2)}, u32[]{:S(2)}) async-start(bf16[128,4,2048]{2,1,0:T(4,128)(2,1)} %convert_element_type.64), calls=%async_computation.5 | async-start | bytes 4194304 | tf_op jit(solution)/shard_map/all_to_all | solution.py:183
  366.1 89.2 %reduce-scatter.5.cloned.1.call-done = f32[256,512]{1,0:T(8,128)} async-done(((f32[2048,512]{1,0:T(8,128)}), f32[256,512]{1,0:T(8,128)}) %reduce-scatter.5.cloned.1.call-update) | async-done | bytes 524304 | tf_op jit(solution)/shard_map/reduce_scatter | solution.py:174
  459.2 8.4 %all-to-all-start.7 = ((bf16[128,4,512]{2,1,0:T(4,128)(2,1)}), bf16[128,4,512]{2,1,0:T(4,128)(2,1)S(1)}, u32[]{:S(2)}, u32[]{:S(2)}) async-start(bf16[128,4,512]{2,1,0:T(4,128)(2,1)} %convert_element_type.68), calls=%async_computation.9 | async-start | bytes 1048576 | tf_op jit(solution)/shard_map/all_to_all | solution.py:197
  467.6 80.6 %reduce-scatter.3.cloned.1.call-done = f32[256,512]{1,0:T(8,128)} async-done(((f32[2048,512]{1,0:T(8,128)}), f32[256,512]{1,0:T(8,128)}) %reduce-scatter.3.cloned.1.call-update) | async-done | bytes 524304 | tf_op jit(solution)/shard_map/reduce_scatter | solution.py:173
  552.2 8.5 %all-to-all-start.6 = ((bf16[128,4,512]{2,1,0:T(4,128)(2,1)}), bf16[128,4,512]{2,1,0:T(4,128)(2,1)S(1)}, u32[]{:S(2)}, u32[]{:S(2)}) async-start(bf16[128,4,512]{2,1,0:T(4,128)(2,1)} %convert_element_type.66), calls=%async_computation.7 | async-start | bytes 1048576 | tf_op jit(solution)/shard_map/all_to_all | solution.py:190
  563.1 5.8 gather_fusion.2
  (223 shorter events, 210.3 us)
Async XLA Ops:
  8.5 70.4 %copy-start.7 = (s32[256]{0:T(256)}, s32[256]{0:T(256)S(1)}, u32[]{:S(2)}) copy-start(s32[256]{0:T(256)S(1)} %compare_select_fusion.4) | copy-start | bytes 3076
  10.6 21.3 %all-to-all-start = ((s32[128,1,4]{2,1,0:T(1,128)}), s32[128,1,4]{2,1,0:T(1,128)S(1)}, u32[]{:S(2)}, u32[]{:S(2)}) async-start(s32[128,1,4]{2,1,0:T(1,128)} %bitcast.4), calls=%async_computation | async-start | bytes 131072 | tf_op jit(solution)/shard_map/all_to_all | solution.py:55
  31.9 18.2 %all-to-all-start.3 = ((bf16[128,4,512]{2,1,0:T(4,128)(2,1)}), bf16[128,4,512]{2,1,0:T(4,128)(2,1)S(1)}, u32[]{:S(2)}, u32[]{:S(2)}) async-start(bf16[128,4,512]{2,1,0:T(4,128)(2,1)} %reshape.384), calls=%async_computation.3 | async-start | bytes 1048576 | tf_op jit(solution)/shard_map/all_to_all | solution.py:53
  50.1 18.0 %all-to-all-start.1 = ((bf16[128,4,512]{2,1,0:T(4,128)(2,1)}), bf16[128,4,512]{2,1,0:T(4,128)(2,1)S(1)}, u32[]{:S(2)}, u32[]{:S(2)}) async-start(bf16[128,4,512]{2,1,0:T(4,128)(2,1)} %reshape.376), calls=%async_computation.1 | async-start | bytes 1048576 | tf_op jit(solution)/shard_map/all_to_all | solution.py:52
  68.1 37.5 %all-to-all-start.2 = ((bf16[128,4,2048]{2,1,0:T(4,128)(2,1)}), bf16[128,4,2048]{2,1,0:T(4,128)(2,1)S(1)}, u32[]{:S(2)}, u32[]{:S(2)}) async-start(bf16[128,4,2048]{2,1,0:T(4,128)(2,1)} %reshape.381), calls=%async_computation.2 | async-start | bytes 4194304 | tf_op jit(solution)/shard_map/all_to_all | solution.py:51
  72.2 110.3 %all-gather.4.cloned.1.call-start = ((), (), s32[]{:S(2)}) async-start(), calls=%async_computation.10 | async-start | bytes 2359296 | tf_op jit(solution)/shard_map/all_gather | solution.py:83
  87.4 23.4 %copy-start.10 = (s32[1,16]{1,0:T(1,128)S(1)}, s32[1,16]{1,0:T(1,128)}, u32[]{:S(2)}) copy-start(s32[1,16]{1,0:T(1,128)} %param.18) | copy-start | bytes 196
  87.4 23.6 %copy-start.9 = (s32[1,256]{1,0:T(1,128)S(1)}, s32[1,256]{1,0:T(1,128)}, u32[]{:S(2)}) copy-start(s32[1,256]{1,0:T(1,128)} %param.19) | copy-start | bytes 3076
  105.6 65.7 %all-to-all-start.4 = ((bf16[128,4,2048]{2,1,0:T(4,128)(2,1)}), bf16[128,4,2048]{2,1,0:T(4,128)(2,1)}, u32[]{:S(2)}, u32[]{:S(2)}) async-start(bf16[128,4,2048]{2,1,0:T(4,128)(2,1)} %reshape.387), calls=%async_computation.4 | async-start | bytes 4194304 | tf_op jit(solution)/shard_map/all_to_all | solution.py:54
  110.7 106.0 %all-gather.6.cloned.1.call-start = ((), (), s32[]{:S(2)}) async-start(), calls=%async_computation.11 | async-start | bytes 2359296 | tf_op jit(solution)/shard_map/all_gather | solution.py:84
  162.4 292.9 %reduce-scatter.5.cloned.1.call-start = ((), (), s32[]{:S(2)}) async-start(), calls=%async_computation.13 | async-start | bytes 4718592 | tf_op jit(solution)/shard_map/reduce_scatter | solution.py:174
  264.8 3.8 copy-start
  264.8 4.1 copy-start.1
  289.9 3.8 copy-start
  289.9 4.1 copy-start.1
  315.0 3.8 copy-start
  315.0 4.1 copy-start.1
  340.1 3.8 copy-start
  340.1 4.1 copy-start.1
  352.1 196.1 %reduce-scatter.3.cloned.1.call-start = ((), (), s32[]{:S(2)}) async-start(), calls=%async_computation.12 | async-start | bytes 4718592 | tf_op jit(solution)/shard_map/reduce_scatter | solution.py:173
  359.3 99.9 %all-to-all-start.5 = ((bf16[128,4,2048]{2,1,0:T(4,128)(2,1)}), bf16[128,4,2048]{2,1,0:T(4,128)(2,1)S(1)}, u32[]{:S(2)}, u32[]{:S(2)}) async-start(bf16[128,4,2048]{2,1,0:T(4,128)(2,1)} %convert_element_type.64), calls=%async_computation.5 | async-start | bytes 4194304 | tf_op jit(solution)/shard_map/all_to_all | solution.py:183
  459.2 93.0 %all-to-all-start.7 = ((bf16[128,4,512]{2,1,0:T(4,128)(2,1)}), bf16[128,4,512]{2,1,0:T(4,128)(2,1)S(1)}, u32[]{:S(2)}, u32[]{:S(2)}) async-start(bf16[128,4,512]{2,1,0:T(4,128)(2,1)} %convert_element_type.68), calls=%async_computation.9 | async-start | bytes 1048576 | tf_op jit(solution)/shard_map/all_to_all | solution.py:197
  551.2 9.4 %copy-start.8 = (s32[256]{0:T(256)S(1)}, s32[256]{0:T(256)}, u32[]{:S(2)}) copy-start(s32[256]{0:T(256)} %copy-done.7) | copy-start | bytes 3076
  552.2 22.5 %all-to-all-start.6 = ((bf16[128,4,512]{2,1,0:T(4,128)(2,1)}), bf16[128,4,512]{2,1,0:T(4,128)(2,1)S(1)}, u32[]{:S(2)}, u32[]{:S(2)}) async-start(bf16[128,4,512]{2,1,0:T(4,128)(2,1)} %convert_element_type.66), calls=%async_computation.7 | async-start | bytes 1048576 | tf_op jit(solution)/shard_map/all_to_all | solution.py:190
  (14 other events, 22.7 us)
Sparse Core Ops, SparseCore 0:
  79.0 73.6 all-gather.3
  162.5 54.1 all-gather.5
  352.2 102.9 reduce-scatter.4
  458.9 89.2 reduce-scatter.2
where the time goes:
time: 594 us; the launch traced here: 583 us
  waiting for transfers between devices  227 us (38%)
  local copies, waits for them, and re-layouts  123 us (21%)
  matrix products  104 us (18%)
  starting transfers between devices  52.6 us (9%)
  blocking collectives  47.5 us (8%)
  between operations  14.4 us (2%)
  other arithmetic  14.2 us (2%)
    reduce_scatter x1, waiting for transfers between devices, local(): lax.psum_scatter(dvalue_all, 'ctx', scatter_dimension=0, tiled=True)  89.2 us
    reduce_scatter x1, waiting for transfers between devices, local(): lax.psum_scatter(dkey_all, 'ctx', scatter_dimension=0, tiled=True)  80.6 us
    all_gather x1, blocking collectives, local(): lax.all_gather(doc_ids[0], 'ctx', axis=0, tiled=True)  47.5 us
    dot_general x4, matrix products, grad_terms(): jnp.einsum('qhgd,khd->hgqk', grad_blk, value_blk, preferred_element_type=...  24 us
    dot_general x4, matrix products, output_step(): jnp.einsum('hgqk,khd->qhgd', probs_low, value_blk, preferred_element_type...  22.4 us
    dot_general x8, matrix products, masked_scores(): jnp.einsum('qhgd,khd->hgqk', query_blk, key_blk, preferred_element_type=j...  18.6 us
    all_to_all x1, waiting for transfers between devices, local(): lax.all_to_all(bucket(query_in, 0), ('dp', 'ctx'), split_axis=0, concat_a...  18.2 us
    scatter x4, local copies, waits for them, and re-layouts, unpack(): return jnp.zeros((local_rows,) + values.shape[1:], values.dtype).at[landi...  17.3 us
  transfers between devices with their start and end apart: 12, of which 8 were waited for; matrix products, arithmetic and copies ran while one was open for 17% of the time, Pallas kernels for 0%

commit v1 on v0

--- a/solution.py
+++ b/solution.py
@@ -38,39 +38,29 @@
     capacity = local_rows // devices + 2
     groups = HQ // HK
     score_scale = DH ** (-0.5)
+    q_cols = query_in.shape[1]
+    k_cols = key_in.shape[1]
     owners = target // local_rows
     onehot = (owners[:, None] == jnp.arange(devices, dtype=jnp.int32)[None, :]).astype(jnp.int32)
     earlier = jnp.cumsum(onehot, axis=0) - onehot
     slot_ids = owners * capacity + jnp.sum(earlier * onehot, axis=1)
 
-    def bucket(values, filler):
-        holder = jnp.full((devices * capacity,) + values.shape[1:], filler, values.dtype)
-        return holder.at[slot_ids].set(values).reshape((devices, capacity) + values.shape[1:])
+    place_col = jnp.zeros((local_rows, 128), jnp.bfloat16).at[:, 0].set(
+        (target % local_rows + 1).astype(jnp.bfloat16)
+    )
+    payload = jnp.concatenate([query_in, key_in, value_in, grad_out, place_col], axis=1)
+    width = payload.shape[1]
+    holder = jnp.zeros((devices * capacity, width), jnp.bfloat16).at[slot_ids].set(payload)
+    got = lax.all_to_all(
+        holder.reshape(devices, capacity, width), ("dp", "ctx"), split_axis=0, concat_axis=0, tiled=True
+    ).reshape(devices * capacity, width)
+    arrived = got[:, 2 * q_cols + 2 * k_cols].astype(jnp.int32) - 1
+    landing = jnp.where(arrived >= 0, arrived, local_rows)
+    rows = jnp.zeros((local_rows, width), jnp.bfloat16).at[landing].set(got, mode="drop")
+    query = rows[:, :q_cols]
+    kv_rows = rows[:, q_cols : q_cols + 2 * k_cols]
+    grad_rows = rows[:, q_cols + 2 * k_cols : 2 * q_cols + 2 * k_cols]
 
-    got_query, got_key, got_value, got_grad, got_place = (
-        lax.all_to_all(bucket(query_in, 0), ("dp", "ctx"), split_axis=0, concat_axis=0, tiled=True),
-        lax.all_to_all(bucket(key_in, 0), ("dp", "ctx"), split_axis=0, concat_axis=0, tiled=True),
-        lax.all_to_all(bucket(value_in, 0), ("dp", "ctx"), split_axis=0, concat_axis=0, tiled=True),
-        lax.all_to_all(bucket(grad_out, 0), ("dp", "ctx"), split_axis=0, concat_axis=0, tiled=True),
-        lax.all_to_all(
-            bucket(target % local_rows, -1), ("dp", "ctx"), split_axis=0, concat_axis=0, tiled=True
-        ),
-    )
-    arrived = got_place.reshape(-1)
-    landing = jnp.where(arrived >= 0, arrived, local_rows)
-
-    def unpack(values):
-        values = values.reshape((devices * capacity,) + values.shape[2:])
-        return (
-            jnp.zeros((local_rows,) + values.shape[1:], values.dtype)
-            .at[landing]
-            .set(values, mode="drop")
-        )
-
-    query = unpack(got_query)
-    key_rows = unpack(got_key)
-    value_rows = unpack(got_value)
-    grad_rows = unpack(got_grad)
     span_rows = local_rows // 2
     span_seq = span_order[0]
     pack_len = local_rows * ctx_size
@@ -79,17 +69,17 @@
     ).reshape(-1)
     ctx_index = lax.axis_index("ctx")
     own_pos = lax.dynamic_slice_in_dim(positions, ctx_index * local_rows, local_rows)
-    keys_all, values_all, seq_docs = (
-        lax.all_gather(key_rows, "ctx", axis=0, tiled=True),
-        lax.all_gather(value_rows, "ctx", axis=0, tiled=True),
-        lax.all_gather(doc_ids[0], "ctx", axis=0, tiled=True),
+    doc_col = jnp.zeros((local_rows, 128), jnp.bfloat16).at[:, 0].set(doc_ids[0].astype(jnp.bfloat16))
+    gathered = lax.all_gather(
+        jnp.concatenate([kv_rows, doc_col], axis=1), "ctx", axis=0, tiled=True
     )
+    seq_docs = gathered[:, 2 * k_cols].astype(jnp.int32)
     doc_all = seq_docs.reshape(2 * ctx_size, span_rows)[span_seq].reshape(-1)
     own_docs = lax.dynamic_slice_in_dim(doc_all, ctx_index * local_rows, local_rows)
     query_heads = query.reshape(local_rows, HK, groups, DH)
     grad_heads = grad_rows.reshape(local_rows, HK, groups, DH)
-    key_heads = keys_all.reshape(pack_len, HK, DH)
-    value_heads = values_all.reshape(pack_len, HK, DH)
+    key_heads = gathered[:, :k_cols].reshape(pack_len, HK, DH)
+    value_heads = gathered[:, k_cols : 2 * k_cols].reshape(pack_len, HK, DH)
     num_blocks = pack_len // block_keys
 
     def key_block(block_index):
@@ -169,44 +159,24 @@
         jnp.zeros((pack_len, HK * DH), jnp.float32),
     )
     dquery, dkey_all, dvalue_all = lax.fori_loop(0, num_blocks, back_step, start_back)
-    dkey_own, dvalue_own = (
-        lax.psum_scatter(dkey_all, "ctx", scatter_dimension=0, tiled=True),
-        lax.psum_scatter(dvalue_all, "ctx", scatter_dimension=0, tiled=True),
+    partial = jnp.concatenate([dkey_all, dvalue_all], axis=1).astype(jnp.bfloat16)
+    summed_kv = jnp.sum(
+        lax.all_to_all(
+            partial.reshape(ctx_size, local_rows, 2 * k_cols), "ctx", split_axis=0, concat_axis=0, tiled=True
+        ).astype(jnp.float32),
+        axis=0,
     )
     dquery_full = (dquery * score_scale).reshape(local_rows, HQ * DH)
     source_rows = jnp.where(arrived >= 0, arrived, 0)
-
-    def outgoing(values):
-        return values[source_rows].reshape((devices, capacity) + values.shape[1:])
-
-    back_query, back_key, back_value = (
-        lax.all_to_all(
-            outgoing(dquery_full).astype(jnp.bfloat16),
-            ("dp", "ctx"),
-            split_axis=0,
-            concat_axis=0,
-            tiled=True,
-        ).astype(jnp.float32),
-        lax.all_to_all(
-            outgoing(dkey_own).astype(jnp.bfloat16),
-            ("dp", "ctx"),
-            split_axis=0,
-            concat_axis=0,
-            tiled=True,
-        ).astype(jnp.float32),
-        lax.all_to_all(
-            outgoing(dvalue_own).astype(jnp.bfloat16),
-            ("dp", "ctx"),
-            split_axis=0,
-            concat_axis=0,
-            tiled=True,
-        ).astype(jnp.float32),
-    )
-
-    def picked(values):
-        return values.reshape((devices * capacity,) + values.shape[2:])[slot_ids]
-
-    return (picked(back_query), picked(back_key), picked(back_value))
+    result = jnp.concatenate([dquery_full.astype(jnp.bfloat16), summed_kv.astype(jnp.bfloat16)], axis=1)
+    back = lax.all_to_all(
+        result[source_rows].reshape(devices, capacity, q_cols + 2 * k_cols),
+        ("dp", "ctx"),
+        split_axis=0,
+        concat_axis=0,
+        tiled=True,
+    ).reshape(devices * capacity, q_cols + 2 * k_cols)[slot_ids].astype(jnp.float32)
+    return (back[:, :q_cols], back[:, q_cols : q_cols + k_cols], back[:, q_cols + k_cols :])
 
 
 def solution(mesh):

time: 594 us -> 508 us (0.86)
  blocking collectives: 47.5 us -> 0 us
  starting transfers between devices: 52.6 us -> 24.3 us
  other arithmetic: 14.2 us -> 29 us
  waiting for transfers between devices: 227 us -> 214 us
  local copies, waits for them, and re-layouts: 123 us -> 115 us
    reduce_scatter x2 -> x0, waiting for transfers between devices: 170 us -> none  [the longest x1 89.2 us: local(): lax.psum_scatter(dvalue_all, 'ctx', scatter_dimension=0, tiled=True)]
    all_to_all x8 -> x3, waiting for transfers between devices: 48.2 us -> 154 us  [the longest x1 64.6 us: local(): lax.all_to_all(holder.reshape(devices, capacity, width), ('dp', 'ctx'), s...]
    all_gather x2 -> x1, waiting for transfers between devices: 8.12 us -> 59.6 us  [local(): lax.all_gather(jnp.concatenate([kv_rows, doc_col], axis=1), 'ctx', axis=0...]
    all_gather x1 -> x0, blocking collectives: 47.5 us -> none  [local(): lax.all_gather(doc_ids[0], 'ctx', axis=0, tiled=True)]
    all_to_all x8 -> x3, starting transfers between devices: 52.4 us -> 24 us  [the longest x1 11.9 us: local(): lax.all_to_all(holder.reshape(devices, capacity, width), ('dp', 'ctx'), s...]
    slice x0 -> x7, local copies, waits for them, and re-layouts: none -> 19.1 us  [the longest x2 8.49 us: local(): value_heads = gathered[:, k_cols:2 * k_cols].reshape(pack_len, HK, DH)]
    scatter x9 -> x2, local copies, waits for them, and re-layouts: 30.7 us -> 18.9 us  [the longest x1 10.4 us: local(): jnp.zeros((local_rows, width), jnp.bfloat16).at[landing]]
    gather x6 -> x2, local copies, waits for them, and re-layouts: 17.8 us -> 6.56 us  [the longest x1 3.85 us: local(): result[source_rows].reshape(devices, capacity, q_cols + 2 * k_cols)]
  transfers between devices with their start and end apart: 12 -> 4, of which waited for: 8 -> 4; matrix products, arithmetic and copies ran while one was open for 17% -> 2% of each run, Pallas kernels for 0% -> 0%
where the time goes in v1:
time: 508 us; the launch traced here: 500 us
  waiting for transfers between devices  214 us (42%)
  local copies, waits for them, and re-layouts  115 us (23%)
  matrix products  102 us (20%)
  other arithmetic  29 us (6%)
  starting transfers between devices  24.3 us (5%)
  between operations  14.8 us (3%)
    all_to_all x1, waiting for transfers between devices, local(): lax.all_to_all(holder.reshape(devices, capacity, width), ('dp', 'ctx'), s...  64.6 us
    all_gather x1, waiting for transfers between devices, local(): lax.all_gather(jnp.concatenate([kv_rows, doc_col], axis=1), 'ctx', axis=0...  59.6 us
    all_to_all x1, waiting for transfers between devices, local(): lax.all_to_all(partial.reshape(ctx_size, local_rows, 2 * k_cols), 'ctx',...  48.7 us
    all_to_all x1, waiting for transfers between devices, local(): lax.all_to_all(result[source_rows].reshape(devices, capacity, q_cols + 2...  40.9 us
    dot_general x4, matrix products, output_step(): jnp.einsum('hgqk,khd->qhgd', probs_low, value_blk, preferred_element_type...  22.3 us
    dot_general x4, matrix products, grad_terms(): jnp.einsum('qhgd,khd->hgqk', grad_blk, value_blk, preferred_element_type=...  21.3 us
    dot_general x8, matrix products, masked_scores(): jnp.einsum('qhgd,khd->hgqk', query_blk, key_blk, preferred_element_type=j...  20.3 us
    dot_general x4, matrix products, back_step(): jnp.einsum('hgqk,qhgd->khd', dscore_low, query_heads, preferred_element_t...  19.7 us
  transfers between devices with their start and end apart: 4, of which 4 were waited for; matrix products, arithmetic and copies ran while one was open for 2% of the time, Pallas kernels for 0%

profile of v1, /device:TPU:1, one launch (start us, length us, event | category | flops | bytes accessed | tf_op | source)
XLA Modules:
  0.0 499.6 jit_solution(9435614256057329827)
XLA Ops:
  17.6 8.6 %scatter_custom_fusion = bf16[512,5248]{1,0:T(8,128)(2,1)} fusion(s32[256]{0:T(256)S(1)} %compare_select_fusion.4, bf16[256,5248]{1,0:T(8,128)(2,1)} %pad_dynamic-update-slice_fusion, bf16[]{:T(256)} %constant.226.clone.1), kind=kCustom, calls=%fused_computation.63 | custom fusion | bytes 5374464 | tf_op jit(solution)/shard_map/scatter | solution.py:53
  26.2 9.4 %reshape.352 = bf16[128,4,5248]{2,1,0:T(4,128)(2,1)} reshape(bf16[512,5248]{1,0:T(8,128)(2,1)} %scatter_custom_fusion) | data formatting | bytes 10747904 | tf_op jit(solution)/shard_map/reshape | solution.py:55
  35.6 11.9 %all-to-all-start = ((bf16[128,4,5248]{2,1,0:T(4,128)(2,1)}), bf16[128,4,5248]{2,1,0:T(4,128)(2,1)}, u32[]{:S(2)}, u32[]{:S(2)}) async-start(bf16[128,4,5248]{2,1,0:T(4,128)(2,1)} %reshape.352), calls=%async_computation | async-start | bytes 10747904 | tf_op jit(solution)/shard_map/all_to_all | solution.py:54
  48.5 64.6 %all-to-all-done = bf16[128,4,5248]{2,1,0:T(4,128)(2,1)} async-done(((bf16[128,4,5248]{2,1,0:T(4,128)(2,1)}), bf16[128,4,5248]{2,1,0:T(4,128)(2,1)}, u32[]{:S(2)}, u32[]{:S(2)}) %all-to-all-start) | async-done | bytes 5373984 | tf_op jit(solution)/shard_map/all_to_all | solution.py:54
  113.1 9.0 %reshape.399 = bf16[512,5248]{1,0:T(8,128)(2,1)} reshape(bf16[128,4,5248]{2,1,0:T(4,128)(2,1)} %all-to-all-done) | data formatting | bytes 10747904 | tf_op jit(solution)/shard_map/reshape | solution.py:56
  123.9 10.4 %scatter_custom_fusion.1 = bf16[256,5248]{1,0:T(8,128)(2,1)S(1)} fusion(s32[512]{0:T(512)S(1)} %get-tuple-element.848, bf16[512,5248]{1,0:T(8,128)(2,1)} %reshape.399, bf16[]{:T(256)} %constant.226.clone.1), kind=kCustom, calls=%fused_computation.68 | custom fusion | bytes 2687488 | tf_op jit(solution)/shard_map/scatter | solution.py:59
  146.8 59.6 %all-gather.2.cloned.1.call-done = bf16[2048,1152]{1,0:T(8,128)(2,1)} async-done(((bf16[256,1152]{1,0:T(8,128)(2,1)}), bf16[2048,1152]{1,0:T(8,128)(2,1)}) %all-gather.2.cloned.1.call-update) | async-done | bytes 4718608 | tf_op jit(solution)/shard_map/all_gather | solution.py:73
  224.8 18.0 %while.50 = (s32[]{:T(128)}, f32[4,4,256]{2,1,0:T(4,128)S(1)}, f32[4,4,256]{2,1,0:T(4,128)S(1)}, s32[2048]{0:T(1024)S(1)}, s32[256]{0:T(256)S(1)}, /*index=5*/s3...) while((s32[]{:T(128)}, f32[4,4,256]{2,1,0:T(4,128)S(1)}, ...), condition=%wide.region_9.10_spmd.clone, body=%wide.region_6.9_spmd.clone.sunk | while | flops 551964672 | bytes 18970824 | solution.py:108
  242.9 23.8 %while.51 = (s32[]{:T(128)}, f32[256,4,4,128]{0,3,2,1:T(8,128)}, bf16[2048,4,128]{0,2,1:T(8,128)(2,1)}, s32[2048]{0:T(1024)S(1)}, s32[256]{0:T(256)S(1)}, /*inde...) while((s32[]{:T(128)}, f32[256,4,4,128]{0,3,2,1:T(8,128)}, ...), condition=%wide.region_11.12_spmd.clone, body=%wide.region_10.11_spmd.clone.sunk | while | flops 1083572224 | bytes 6586060 | solution.py:120
  243.3 5.0 %bitcast_add_fusion.4 = f32[256,4,4,128]{0,3,2,1:T(8,128)} fusion(f32[256,4,4,128]{0,3,2,1:T(8,128)} %get-tuple-element.1188, f32[4,4,256]{2,1,0:T(4,128)S(1)} %get-tuple-element.1210, pred[256,512]{0,1:T(8,128)(4,1)S(1)} %compare_and_fusion.7, bf16[256,4,4,128]{3,0,2,1:T(8,128)(2,1)S(1)} %get-tuple-element.1209, pred[]{:T(512)S(6)} %compare.35, ...), kind=kOutput, calls=%fused_computation.26.clone.1 | convolution fusion | flops 1083179008 | bytes 6440448 | tf_op jit(solution)/shard_map/while/body/eval_jaxpr/hgqk,khd->qhgd/dot_general | solution.py:116
  248.7 5.8 %bitcast_add_fusion.4 = f32[256,4,4,128]{0,3,2,1:T(8,128)} fusion(f32[256,4,4,128]{0,3,2,1:T(8,128)} %get-tuple-element.1188, f32[4,4,256]{2,1,0:T(4,128)S(1)} %get-tuple-element.1210, pred[256,512]{0,1:T(8,128)(4,1)S(1)} %compare_and_fusion.7, bf16[256,4,4,128]{3,0,2,1:T(8,128)(2,1)S(1)} %get-tuple-element.1209, pred[]{:T(512)S(6)} %compare.35, ...), kind=kOutput, calls=%fused_computation.26.clone.1 | convolution fusion | flops 1083179008 | bytes 6440448 | tf_op jit(solution)/shard_map/while/body/eval_jaxpr/hgqk,khd->qhgd/dot_general | solution.py:116
  254.8 5.8 %bitcast_add_fusion.4 = f32[256,4,4,128]{0,3,2,1:T(8,128)} fusion(f32[256,4,4,128]{0,3,2,1:T(8,128)} %get-tuple-element.1188, f32[4,4,256]{2,1,0:T(4,128)S(1)} %get-tuple-element.1210, pred[256,512]{0,1:T(8,128)(4,1)S(1)} %compare_and_fusion.7, bf16[256,4,4,128]{3,0,2,1:T(8,128)(2,1)S(1)} %get-tuple-element.1209, pred[]{:T(512)S(6)} %compare.35, ...), kind=kOutput, calls=%fused_computation.26.clone.1 | convolution fusion | flops 1083179008 | bytes 6440448 | tf_op jit(solution)/shard_map/while/body/eval_jaxpr/hgqk,khd->qhgd/dot_general | solution.py:116
  260.9 5.8 %bitcast_add_fusion.4 = f32[256,4,4,128]{0,3,2,1:T(8,128)} fusion(f32[256,4,4,128]{0,3,2,1:T(8,128)} %get-tuple-element.1188, f32[4,4,256]{2,1,0:T(4,128)S(1)} %get-tuple-element.1210, pred[256,512]{0,1:T(8,128)(4,1)S(1)} %compare_and_fusion.7, bf16[256,4,4,128]{3,0,2,1:T(8,128)(2,1)S(1)} %get-tuple-element.1209, pred[]{:T(512)S(6)} %compare.35, ...), kind=kOutput, calls=%fused_computation.26.clone.1 | convolution fusion | flops 1083179008 | bytes 6440448 | tf_op jit(solution)/shard_map/while/body/eval_jaxpr/hgqk,khd->qhgd/dot_general | solution.py:116
  271.8 82.3 %while.52 = (s32[]{:T(128)}, f32[256,4,4,128]{0,3,2,1:T(8,128)S(1)}, bf16[2048,512]{1,0:T(8,128)(2,1)}, bf16[2048,512]{1,0:T(8,128)(2,1)}, bf16[2048,4,128]{2,0,...) while((s32[]{:T(128)}, ...), condition=%wide.region_14.15_spmd.clone, body=%wide.region_13.14_spmd.clone.sunk | while | flops 2707292160 | bytes 74381608 | solution.py:161
  277.4 5.3 %fusion.118 = bf16[4,4,256,512]{2,3,1,0:T(8,128)(2,1)} fusion(f32[4,512,256,4]{2,1,3,0:T(8,128)S(1)} %fusion.117, f32[4,4,256]{2,1,0:T(4,128)S(1)} %get-tuple-element.1264, f32[4,4,256]{2,1,0:T(4,128)S(1)} %get-tuple-element.1261, pred[256,512]{0,1:T(8,128)(4,1)S(1)} %compare_and_fusion.8, bf16[256,4,4,128]{0,3,2,1:T(8,128)(2,1)S(1)} %copy-done.3, ...), kind=kOutput, calls=%fused_computation.37.clone.1 | convolution fusion | flops 549453824 | bytes 14319620 | tf_op jit(solution)/shard_map/while/body/eval_jaxpr/qhgd,khd->hgqk/dot_general | solution.py:29
  282.9 4.9 fusion.120
  297.9 5.3 %fusion.118 = bf16[4,4,256,512]{2,3,1,0:T(8,128)(2,1)} fusion(f32[4,512,256,4]{2,1,3,0:T(8,128)S(1)} %fusion.117, f32[4,4,256]{2,1,0:T(4,128)S(1)} %get-tuple-element.1264, f32[4,4,256]{2,1,0:T(4,128)S(1)} %get-tuple-element.1261, pred[256,512]{0,1:T(8,128)(4,1)S(1)} %compare_and_fusion.8, bf16[256,4,4,128]{0,3,2,1:T(8,128)(2,1)S(1)} %copy-done.3, ...), kind=kOutput, calls=%fused_computation.37.clone.1 | convolution fusion | flops 549453824 | bytes 14319620 | tf_op jit(solution)/shard_map/while/body/eval_jaxpr/qhgd,khd->hgqk/dot_general | solution.py:29
  318.4 5.3 %fusion.118 = bf16[4,4,256,512]{2,3,1,0:T(8,128)(2,1)} fusion(f32[4,512,256,4]{2,1,3,0:T(8,128)S(1)} %fusion.117, f32[4,4,256]{2,1,0:T(4,128)S(1)} %get-tuple-element.1264, f32[4,4,256]{2,1,0:T(4,128)S(1)} %get-tuple-element.1261, pred[256,512]{0,1:T(8,128)(4,1)S(1)} %compare_and_fusion.8, bf16[256,4,4,128]{0,3,2,1:T(8,128)(2,1)S(1)} %copy-done.3, ...), kind=kOutput, calls=%fused_computation.37.clone.1 | convolution fusion | flops 549453824 | bytes 14319620 | tf_op jit(solution)/shard_map/while/body/eval_jaxpr/qhgd,khd->hgqk/dot_general | solution.py:29
  338.9 5.3 %fusion.118 = bf16[4,4,256,512]{2,3,1,0:T(8,128)(2,1)} fusion(f32[4,512,256,4]{2,1,3,0:T(8,128)S(1)} %fusion.117, f32[4,4,256]{2,1,0:T(4,128)S(1)} %get-tuple-element.1264, f32[4,4,256]{2,1,0:T(4,128)S(1)} %get-tuple-element.1261, pred[256,512]{0,1:T(8,128)(4,1)S(1)} %compare_and_fusion.8, bf16[256,4,4,128]{0,3,2,1:T(8,128)(2,1)S(1)} %copy-done.3, ...), kind=kOutput, calls=%fused_computation.37.clone.1 | convolution fusion | flops 549453824 | bytes 14319620 | tf_op jit(solution)/shard_map/while/body/eval_jaxpr/qhgd,khd->hgqk/dot_general | solution.py:29
  358.7 6.4 %copy.114 = bf16[8,256,1024]{1,2,0:T(8,128)(2,1)} copy(bf16[8,256,1024]{2,1,0:T(8,128)(2,1)} %pad_maximum_fusion) | data formatting | bytes 8388608 | tf_op jit(solution)/shard_map/concatenate | solution.py:162
  370.8 48.7 %all-to-all-done.1 = bf16[8,256,1024]{1,2,0:T(8,128)(2,1)} async-done(((bf16[8,256,1024]{1,2,0:T(8,128)(2,1)}), bf16[8,256,1024]{1,2,0:T(8,128)(2,1)}, u32[]{:S(2)}, u32[]{:S(2)}) %all-to-all-start.1) | async-done | bytes 4194336 | tf_op jit(solution)/shard_map/all_to_all | solution.py:164
  426.7 6.1 %reshape.360 = bf16[128,4,3072]{2,1,0:T(4,128)(2,1)} reshape(bf16[512,3072]{1,0:T(8,128)(2,1)} %gather_fusion.1) | data formatting | bytes 6291456 | tf_op jit(solution)/shard_map/reshape | solution.py:173
  432.8 7.5 %all-to-all-start.2 = ((bf16[128,4,3072]{2,1,0:T(4,128)(2,1)}), bf16[128,4,3072]{2,1,0:T(4,128)(2,1)}, u32[]{:S(2)}, u32[]{:S(2)}) async-start(bf16[128,4,3072]{2,1,0:T(4,128)(2,1)} %reshape.360), calls=%async_computation.2 | async-start | bytes 6291456 | tf_op jit(solution)/shard_map/all_to_all | solution.py:172
  440.4 40.9 %all-to-all-done.2 = bf16[128,4,3072]{2,1,0:T(4,128)(2,1)} async-done(((bf16[128,4,3072]{2,1,0:T(4,128)(2,1)}), bf16[128,4,3072]{2,1,0:T(4,128)(2,1)}, u32[]{:S(2)}, u32[]{:S(2)}) %all-to-all-start.2) | async-done | bytes 3145760 | tf_op jit(solution)/shard_map/all_to_all | solution.py:172
  (185 shorter events, 152.4 us)
Async XLA Ops:
  7.2 7.2 %copy-start.5 = (bf16[256,512]{1,0:T(8,128)(2,1)S(1)}, bf16[256,512]{1,0:T(8,128)(2,1)}, u32[]{:S(2)}) copy-start(bf16[256,512]{1,0:T(8,128)(2,1)} %param.18) | copy-start | bytes 786436
  7.2 7.9 %copy-start.6 = (bf16[256,512]{1,0:T(8,128)(2,1)S(1)}, bf16[256,512]{1,0:T(8,128)(2,1)}, u32[]{:S(2)}) copy-start(bf16[256,512]{1,0:T(8,128)(2,1)} %param.19) | copy-start | bytes 786436
  7.2 8.7 %copy-start.4 = (bf16[256,2048]{1,0:T(8,128)(2,1)S(1)}, bf16[256,2048]{1,0:T(8,128)(2,1)}, u32[]{:S(2)}) copy-start(bf16[256,2048]{1,0:T(8,128)(2,1)} %param.20) | copy-start | bytes 3145732
  11.9 5.6 %copy-start.8 = (s32[256]{0:T(256)}, s32[256]{0:T(256)S(1)}, u32[]{:S(2)}) copy-start(s32[256]{0:T(256)S(1)} %compare_select_fusion.4) | copy-start | bytes 3076
  35.6 12.1 %copy-start.10 = (s32[1,256]{1,0:T(1,128)S(1)}, s32[1,256]{1,0:T(1,128)}, u32[]{:S(2)}) copy-start(s32[1,256]{1,0:T(1,128)} %param.23) | copy-start | bytes 3076
  35.6 77.5 %all-to-all-start = ((bf16[128,4,5248]{2,1,0:T(4,128)(2,1)}), bf16[128,4,5248]{2,1,0:T(4,128)(2,1)}, u32[]{:S(2)}, u32[]{:S(2)}) async-start(bf16[128,4,5248]{2,1,0:T(4,128)(2,1)} %reshape.352), calls=%async_computation | async-start | bytes 10747904 | tf_op jit(solution)/shard_map/all_to_all | solution.py:54
  47.5 158.9 %all-gather.2.cloned.1.call-start = ((), (), s32[]{:S(2)}) async-start(), calls=%async_computation.3 | async-start | bytes 5308416 | tf_op jit(solution)/shard_map/all_gather | solution.py:73
  123.9 12.1 %copy-start.11 = (s32[1,16]{1,0:T(1,128)S(1)}, s32[1,16]{1,0:T(1,128)}, u32[]{:S(2)}) copy-start(s32[1,16]{1,0:T(1,128)} %param.22) | copy-start | bytes 196
  134.2 1.7 copy-start.2
  272.4 2.7 copy-start.3
  282.9 4.9 copy-start
  292.9 2.7 copy-start.3
  303.4 4.9 copy-start
  313.4 2.7 copy-start.3
  323.9 4.9 copy-start
  333.9 2.7 copy-start.3
  344.4 4.9 copy-start
  365.2 4.7 copy-start.7
  365.2 54.3 %all-to-all-start.1 = ((bf16[8,256,1024]{1,2,0:T(8,128)(2,1)}), bf16[8,256,1024]{1,2,0:T(8,128)(2,1)}, u32[]{:S(2)}, u32[]{:S(2)}) async-start(bf16[8,256,1024]{1,2,0:T(8,128)(2,1)} %copy.114), calls=%async_computation.1 | async-start | bytes 8388608 | tf_op jit(solution)/shard_map/all_to_all | solution.py:164
  432.8 7.5 %copy-start.9 = (s32[256]{0:T(256)S(1)}, s32[256]{0:T(256)}, u32[]{:S(2)}) copy-start(s32[256]{0:T(256)} %copy-done.8) | copy-start | bytes 3076
  432.8 48.4 %all-to-all-start.2 = ((bf16[128,4,3072]{2,1,0:T(4,128)(2,1)}), bf16[128,4,3072]{2,1,0:T(4,128)(2,1)}, u32[]{:S(2)}, u32[]{:S(2)}) async-start(bf16[128,4,3072]{2,1,0:T(4,128)(2,1)} %reshape.360), calls=%async_computation.2 | async-start | bytes 6291456 | tf_op jit(solution)/shard_map/all_to_all | solution.py:172
  488.5 2.3 copy-start.1
Sparse Core Ops, SparseCore 0:
  135.4 70.8 all-gather.1
